TPU v7x, 256 devices: a whole 4x4x8 slice. The times are simulated.
256 devices in a mesh: ctx: 64 (over y, z, core), tp: 4 (over x).
Axes of the slice: x: 4, y: 4, z: 8, core: 2. Of those that a mesh axis runs over, the one named last changes fastest.
Arguments:
- queries: bfloat16 [32768, 4096], P('ctx', 'tp'), may hold values from -160 to 160
- keys: bfloat16 [32768, 512], P('ctx', 'tp'), may hold values from -5 to 5
- values: bfloat16 [32768, 512], P('ctx', 'tp'), may hold values from -6.5 to 6.5
- evicted: int32 [32768, 4], P('ctx', 'tp'), may hold values 0 or 1
- block_lists: int32 [256, 2], P('ctx'), may hold values from 0 to 6, as said below
- map_query: bfloat16 [4, 128, 64], P('tp'), may hold values from -0.5 to 0.5
- map_key: bfloat16 [4, 128, 64], P('tp'), may hold values from -0.5 to 0.5
- state_gain: float32 [4], P('tp'), may hold values from 0.001953125 to 0.0078125
- out_weight: bfloat16 [4096, 8192], P('tp', 'ctx'), may hold values from -0.09375 to 0.09375
Outputs:
- layer_out: bfloat16 [32768, 8192], P('ctx', 'tp')
Inputs may be any that keep to these rules, and one draw needn't show every extreme that they name: `block_lists`: query block b with local index i = b % (4) lists entry 0 = 4 + i - 1 and entry 1 in 0 to 4 + i - 2, so the two entries differ and lie before the diagonal block.
All inputs are finite; a program needn't handle non-finite values. No bound on the sum of `evicted` on one device may be relied on, other than what follows from the above.
Results may differ from a plain program's by a relative error of at most 0.012.
Values may be sent and summed in bfloat16 or wider, within the bound.
No kernel may reach another device: no remote copies, remote signals or barrier semaphores. Data moves between devices by JAX's collectives and lax.ppermute only.
A program may use at most 128 MiB of HBM per device.

v0:
```python
import jax
import jax.numpy as jnp
from jax import lax
from jax.sharding import Mesh
from jax.sharding import PartitionSpec as P

CTX = ("ctx_0", "ctx_1", "ctx_2")


def passed_along(block, axis, distance):
    devices = range(lax.axis_size(axis))
    route = [(i - distance, i) for i in devices if i - distance in devices]
    return lax.ppermute(block, axis, route)


def neutral_like(shard, identity):
    return jax.tree.map(
        lambda a, e: jnp.broadcast_to(jnp.asarray(e, a.dtype), a.shape), shard, identity
    )


def all_in_one(shard, axis):
    leaves = jax.tree.leaves(shard)
    order = sorted(range(len(leaves)), key=lambda k: -leaves[k].size)
    width = (1, *leaves[order[0]].shape)[-1]
    lines = [
        jnp.pad(leaves[k].reshape(-1), (0, -leaves[k].size % width)).reshape(-1, width)
        for k in order
    ]
    both, at, found = (lax.all_gather(jnp.concatenate(lines), axis), 0, {})
    for k, line in zip(order, lines):
        slab = both[:, at : at + len(line)].reshape(len(both), -1)
        found[k] = slab[:, : leaves[k].size].reshape(-1, *leaves[k].shape)
        at += len(line)
    numbers = iter(range(len(leaves)))
    return jax.tree.map(lambda _: found[next(numbers)], shard)


def carried_in(shard, axes, combine, identity):
    before = start = neutral_like(shard, identity)
    running = shard
    for axis in reversed(axes):
        devices, here = (lax.axis_size(axis), lax.axis_index(axis))
        pieces = all_in_one(
            jax.tree.map(
                lambda part, kind: part.astype(kind), running, (jnp.bfloat16, jnp.bfloat16)
            ),
            axis,
        )
        inside, running = (start, start)
        for k in range(devices):
            passed = k < here
            running = combine(
                running, jax.tree.map(lambda part, own: part[k].astype(own.dtype), pieces, shard)
            )
            inside = jax.tree.map(lambda new, old: jnp.where(passed, new, old), running, inside)
        before = combine(inside, before)
    return before


def feature(inputs, kernel):
    return jax.nn.elu(jnp.dot(inputs, kernel, preferred_element_type=jnp.float32)) + 1.0


def add_pair(earlier, later):
    return (earlier[0] + later[0], earlier[1] + later[1])


def body(queries, keys, values, evicted, block_lists, map_query, map_key, state_gain, out_weight):
    tok_rows = keys.shape[0]
    groups_here = map_key.shape[0]
    head_dim = map_key.shape[1]
    blocks_dev = block_lists.shape[0]
    block_rows = tok_rows // blocks_dev
    group_size = queries.shape[1] // (groups_here * head_dim)
    highest = lax.Precision.HIGHEST
    device = lax.axis_index(CTX)
    width_kv = groups_here * head_dim
    neighbour = passed_along(jnp.concatenate([keys, values], axis=1), CTX, 1)
    left_keys = neighbour[:, :width_kv]
    left_values = neighbour[:, width_kv:]
    group = 0
    key_feats = feature(keys, map_key[group]) * evicted.astype(jnp.float32)
    state_terms = [
        jnp.einsum("tr,th->rh", key_feats, values.astype(jnp.float32), precision=highest)
    ]
    norm_terms = [jnp.sum(key_feats, axis=0)]
    totals = jnp.stack(state_terms)
    counts = jnp.stack(norm_terms)
    packed = jnp.concatenate(
        [totals[0], jnp.pad(counts, ((0, 0), (0, totals.shape[2] - counts.shape[1])))], axis=0
    ).astype(jnp.float32)
    before = jnp.zeros_like(packed)
    running = packed
    for axis in reversed(CTX):
        size, here = (lax.axis_size(axis), lax.axis_index(axis))
        whole = running
        for shift in range(1, size):
            arrived = lax.ppermute(running, axis, [(i, (i + shift) % size) for i in range(size)])
            before = before + jnp.where(shift <= here, arrived, 0.0)
            whole = whole + arrived
        running = whole
    states = before[None, : totals.shape[1]]
    norms = before[None, totals.shape[1], : counts.shape[1]]
    scale = head_dim ** (-0.5)
    offsets = jnp.arange(block_rows, dtype=jnp.int32)
    group = 0
    window_keys = jnp.concatenate([left_keys, keys], axis=0).reshape(
        2 * blocks_dev, block_rows, head_dim
    )
    window_values = jnp.concatenate([left_values, values], axis=0).reshape(
        2 * blocks_dev, block_rows, head_dim
    )
    query_group = queries.reshape(tok_rows, group_size, head_dim)
    query_feats = feature(query_group, map_query[group])
    reads = jnp.einsum("qhr,rd->qhd", query_feats, states[group], precision=highest)
    mass = jnp.einsum("qhr,r->qh", query_feats, norms[group], precision=highest)
    row_pieces = []
    for local in range(blocks_dev):
        chosen = jnp.concatenate(
            [block_lists[local], jnp.full((1,), blocks_dev + local, jnp.int32)]
        )
        key_rows = jnp.take(window_keys, chosen, axis=0).reshape(-1, head_dim)
        value_rows = jnp.take(window_values, chosen, axis=0).reshape(-1, head_dim)
        positions = (
            ((device - 1) * tok_rows + chosen * block_rows)[:, None] + offsets[None, :]
        ).reshape(-1)
        query_pos = device * tok_rows + local * block_rows + offsets
        valid = (positions[None, :] >= 0) & (positions[None, :] <= query_pos[:, None])
        rows_here = slice(local * block_rows, (local + 1) * block_rows)
        query = query_group[rows_here]
        scores = (
            jnp.einsum("qhd,kd->qhk", query, key_rows, preferred_element_type=jnp.float32) * scale
        )
        scores = jnp.where(valid[:, None, :], scores, -jnp.inf)
        top = jnp.max(scores, axis=2)
        weights = jnp.exp(scores - top[:, :, None])
        total = jnp.sum(weights, axis=2)
        probs = weights.astype(jnp.bfloat16)
        numer = jnp.einsum("qhk,kd->qhd", probs, value_rows, preferred_element_type=jnp.float32)
        damping = jnp.exp(-top) * state_gain[group]
        mixed = (numer + damping[:, :, None] * reads[rows_here]) / (
            total + damping * mass[rows_here]
        )[:, :, None]
        row_pieces.append(mixed.reshape(block_rows, group_size * head_dim).astype(jnp.bfloat16))
    group_cols = jnp.concatenate(row_pieces, axis=0)
    n_tp = lax.axis_size("tp")
    swap = [
        (rows * n_tp + group, (rows - group) % n_tp * n_tp + rows)
        for group in range(n_tp)
        for rows in range(n_tp)
    ]
    moved = lax.ppermute(out_weight, ("ctx_0", "tp"), swap)
    gathered = lax.all_gather(moved, CTX, axis=1, tiled=True)
    width = gathered.shape[1] // n_tp
    summed = None
    for shift in range(n_tp):
        if shift == 0:
            rows_in = group_cols
        else:
            rows_in = lax.ppermute(group_cols, "tp", [(i, (i + shift) % n_tp) for i in range(n_tp)])
        term = jnp.dot(
            rows_in,
            gathered[:, shift * width : (shift + 1) * width],
            preferred_element_type=jnp.float32,
        )
        summed = term if summed is None else summed + term
    return summed.astype(jnp.bfloat16)


def solution(mesh):
    finer = Mesh(mesh.devices.reshape(4, 8, 2, mesh.shape["tp"]), ("ctx_0", "ctx_1", "ctx_2", "tp"))
    placed = (
        P(CTX, "tp"),
        P(CTX, "tp"),
        P(CTX, "tp"),
        P(CTX, "tp"),
        P(CTX, None),
        P("tp", None, None),
        P("tp", None, None),
        P("tp"),
        P("tp", CTX),
    )
    return jax.shard_map(body, mesh=finer, in_specs=placed, out_specs=P(CTX, "tp"), check_vma=False)
```

profile of v0, /device:TPU:1, one launch (start us, length us, event | category | flops | bytes accessed | tf_op | source)
XLA Modules:
  0.0 166.2 jit_solution(2092512514743972706)
XLA Ops:
  6.5 1.7 %collective-permute-start.12 = (bf16[1024,128]{1,0:T(8,128)(2,1)}, bf16[1024,128]{1,0:T(8,128)(2,1)S(1)}, u32[]{:S(2)}, u32[]{:S(2)}) collective-permute-start(bf16[1024,128]{1,0:T(8,128)(2,1)} %param.19), channel_id=1, source_target_pairs={{0,0},{64,65},{128,130},{192,195},{1,192},{65,1},{129,66},{193,131... | collective-permute-start | bytes 786440 | tf_op jit(solution)/shard_map/ppermute | solution.py:153
  12.1 3.3 %collective-permute-start.1 = (f32[65,128]{1,0:T(8,128)S(1)}, f32[65,128]{1,0:T(8,128)S(1)}, u32[]{:S(2)}, u32[]{:S(2)}) collective-permute-start(f32[65,128]{1,0:T(8,128)S(1)} %select_maximum_fusion), channel_id=1, source_target_pairs={{0,4},{4,0},{1,5},{5,1},{2,6},{6,2},{3,7},{7,3},{8,12},{12,8},{9,1... | collective-permute-start | bytes 99848 | tf_op jit(solution)/shard_map/ppermute | solution.py:99
  17.9 1.7 %pad_maximum_fusion.1 = bf16[512,256]{1,0:T(8,128)(2,1)} fusion(bf16[512,128]{1,0:T(8,128)(2,1)} %param.13, bf16[512,128]{1,0:T(8,128)(2,1)} %param.12), kind=kLoop, calls=%fused_computation.74 | loop fusion | flops 524288 | bytes 524288 | tf_op jit(solution)/shard_map/concatenate | solution.py:79
  24.5 3.9 %collective-permute-start.8 = (f32[65,128]{1,0:T(8,128)S(1)}, f32[65,128]{1,0:T(8,128)S(1)}, u32[]{:S(2)}, u32[]{:S(2)}) collective-permute-start(f32[65,128]{1,0:T(8,128)S(1)} %fusion.76), channel_id=1, source_target_pairs={{0,56},{8,0},{16,8},{24,16},{32,24},{40,32},{48,40},{56,48},{1,57}... | collective-permute-start | bytes 99848 | tf_op jit(solution)/shard_map/ppermute | solution.py:99
  30.8 4.5 %collective-permute-start.5 = (f32[65,128]{1,0:T(8,128)S(1)}, f32[65,128]{1,0:T(8,128)S(1)}, u32[]{:S(2)}, u32[]{:S(2)}) collective-permute-start(f32[65,128]{1,0:T(8,128)S(1)} %fusion.76), channel_id=1, source_target_pairs={{0,32},{8,40},{16,48},{24,56},{32,0},{40,8},{48,16},{56,24},{1,33}... | collective-permute-start | bytes 99848 | tf_op jit(solution)/shard_map/ppermute | solution.py:99
  35.3 2.2 %collective-permute-start.3 = (f32[65,128]{1,0:T(8,128)S(1)}, f32[65,128]{1,0:T(8,128)S(1)}, u32[]{:S(2)}, u32[]{:S(2)}) collective-permute-start(f32[65,128]{1,0:T(8,128)S(1)} %fusion.76), channel_id=1, source_target_pairs={{0,16},{8,24},{16,32},{24,40},{32,48},{40,56},{48,0},{56,8},{1,17}... | collective-permute-start | bytes 99848 | tf_op jit(solution)/shard_map/ppermute | solution.py:99
  37.4 1.4 collective-permute-start.2
  39.4 4.5 %collective-permute-start = (bf16[512,256]{1,0:T(8,128)(2,1)}, bf16[512,256]{1,0:T(8,128)(2,1)}, u32[]{:S(2)}, u32[]{:S(2)}) collective-permute-start(bf16[512,256]{1,0:T(8,128)(2,1)} %pad_maximum_fusion.1), channel_id=1, source_target_pairs={{0,4},{4,8},{8,12},{12,16},{16,20},{20,24},{24,28},{28,32},{32,36}... | collective-permute-start | bytes 786440 | tf_op jit(solution)/shard_map/ppermute | solution.py:13
  44.0 18.8 %collective-permute-start.11 = (f32[65,128]{1,0:T(8,128)S(1)}, f32[65,128]{1,0:T(8,128)S(1)}, u32[]{:S(2)}, u32[]{:S(2)}) collective-permute-start(f32[65,128]{1,0:T(8,128)S(1)} %add_add_fusion), channel_id=1, source_target_pairs={{0,192},{64,0},{128,64},{192,128},{1,193},{65,1},{129,65},{193,129... | collective-permute-start | bytes 99848 | tf_op jit(solution)/shard_map/ppermute | solution.py:99
  62.8 1.7 %collective-permute-start.10 = (f32[65,128]{1,0:T(8,128)S(1)}, f32[65,128]{1,0:T(8,128)S(1)}, u32[]{:S(2)}, u32[]{:S(2)}) collective-permute-start(f32[65,128]{1,0:T(8,128)S(1)} %add_add_fusion), channel_id=1, source_target_pairs={{0,128},{64,192},{128,0},{192,64},{1,129},{65,193},{129,1},{193,65... | collective-permute-start | bytes 99848 | tf_op jit(solution)/shard_map/ppermute | solution.py:99
  69.8 3.7 %fusion.39 = f32[1,512,8]{0,1,2:T(8,128)S(1)} fusion(f32[512,8,64]{0,2,1:T(8,128)S(1)} %get-tuple-element.49, u8[512,64]{0,1:T(8,128)(4,1)S(1)} %get-tuple-element.48, f32[65,128]{1,0:T(8,128)S(1)} %select_add_fusion), kind=kOutput, calls=%fused_computation.59 | convolution fusion | flops 4980736 | bytes 1098240 | tf_op jit(solution)/shard_map/qhr,r->qh/dot_general | solution.py:117
  74.7 3.2 %fusion.41 = f32[512,8,128]{0,2,1:T(8,128)S(1)} fusion(f32[512,8,64]{0,2,1:T(8,128)S(1)} %get-tuple-element.49, u8[512,64]{0,1:T(8,128)(4,1)} %copy-done.10, f32[65,128]{1,0:T(8,128)} %copy-done.15), kind=kOutput, calls=%fused_computation.60 | convolution fusion | flops 404488192 | bytes 3211264 | tf_op jit(solution)/shard_map/qhr,rd->qhd/dot_general | solution.py:116
  79.0 1.5 gather_fusion.6
  80.4 1.3 gather_fusion.4
  81.8 1.3 gather_fusion.7
  83.8 1.3 gather_fusion.2
  85.1 1.3 gather_fusion.3
  96.1 2.8 %collective-permute-start.14 = (bf16[512,1024]{0,1:T(8,128)(2,1)S(1)}, bf16[512,1024]{0,1:T(8,128)(2,1)}, u32[]{:S(2)}, u32[]{:S(2)}) collective-permute-start(bf16[512,1024]{0,1:T(8,128)(2,1)S(1)} %pad_maximum_fusion), channel_id=1, source_target_pairs={{0,2},{1,3},{2,0},{3,1},{4,6},{5,7},{6,4},{7,5},{8,10},{9,11},{10,... | collective-permute-start | bytes 3145736 | tf_op jit(solution)/shard_map/ppermute | solution.py:161
  98.9 19.9 %collective-permute-done.13 = bf16[512,1024]{0,1:T(8,128)(2,1)} collective-permute-done((bf16[512,1024]{0,1:T(8,128)(2,1)S(1)}, bf16[512,1024]{0,1:T(8,128)(2,1)}, u32[]{:S(2)}, u32[]{:S(2)}) %collective-permute-start.13) | collective-permute-done | bytes 1048608 | tf_op jit(solution)/shard_map/ppermute | solution.py:161
  118.8 20.0 %all-gather.2.cloned.1.call-done = bf16[1024,8192]{1,0:T(8,128)(2,1)} async-done(((bf16[1024,128]{1,0:T(8,128)(2,1)}), bf16[1024,8192]{1,0:T(8,128)(2,1)}) %all-gather.2.cloned.1.call-update) | async-done | bytes 16777232 | tf_op jit(solution)/shard_map/all_gather | solution.py:154
  138.8 4.9 %fusion.4 = f32[512,2048]{1,0:T(8,128)S(1)} fusion(bf16[512,1024]{0,1:T(8,128)(2,1)} %collective-permute-done.13, bf16[1024,8192]{1,0:T(8,128)(2,1)} %all-gather.2.cloned.1.call-done), kind=kOutput, calls=%fused_computation.12 | convolution fusion | flops 2147483648 | bytes 9437184 | tf_op jit(solution)/shard_map/dot_general | solution.py:162
  143.7 4.9 %fusion.2 = f32[512,2048]{1,0:T(8,128)S(1)} fusion(bf16[512,1024]{0,1:T(8,128)(2,1)} %collective-permute-done.14, bf16[1024,8192]{1,0:T(8,128)(2,1)} %all-gather.2.cloned.1.call-done), kind=kOutput, calls=%fused_computation.10 | convolution fusion | flops 2147483648 | bytes 9437184 | tf_op jit(solution)/shard_map/dot_general | solution.py:162
  148.6 4.6 %fusion.6 = f32[512,2048]{1,0:T(8,128)S(1)} fusion(bf16[1024,8192]{1,0:T(8,128)(2,1)} %all-gather.2.cloned.1.call-done, bf16[128,1024]{0,1:T(8,128)(2,1)S(1)} %bitcast.129, bf16[128,1024]{0,1:T(8,128)(2,1)S(1)} %bitcast.127, bf16[128,1024]{0,1:T(8,128)(2,1)S(1)} %bitcast.125, bf16[128,1024]{0,1:T(8,128)(2,1)S(1)} %bitcast.131), kind=kOutput, calls=%fused_computation.14 | convolution fusion | flops 2151677952 | bytes 9437184 | tf_op jit(solution)/shard_map/dot_general | solution.py:162
  153.2 6.2 %add_convert_fusion = bf16[512,2048]{1,0:T(8,128)(2,1)} fusion(f32[512,2048]{1,0:T(8,128)S(1)} %fusion.2, f32[512,2048]{1,0:T(8,128)S(1)} %fusion.6, f32[512,2048]{1,0:T(8,128)S(1)} %fusion.4, bf16[512,1024]{0,1:T(8,128)(2,1)S(1)} %collective-permute-done.15, bf16[1024,8192]{1,0:T(8,128)(2,1)} %all-gather.2.cloned.1.call-done), kind=kOutput, calls=%fused_computation.16 | convolution fusion | flops 2151677952 | bytes 19922944 | tf_op jit(solution)/shard_map/dot_general | solution.py:162
  (126 shorter events, 31.1 us)
Async XLA Ops:
  6.5 16.8 %copy-start = (bf16[1,128,64]{1,2,0:T(8,128)(2,1)S(1)}, bf16[1,128,64]{1,2,0:T(8,128)(2,1)}, u32[]{:S(2)}) copy-start(bf16[1,128,64]{1,2,0:T(8,128)(2,1)} %param.16) | copy-start | bytes 49156
  6.5 16.8 %copy-start.1 = (bf16[512,1024]{1,0:T(8,128)(2,1)S(1)}, bf16[512,1024]{1,0:T(8,128)(2,1)}, u32[]{:S(2)}) copy-start(bf16[512,1024]{1,0:T(8,128)(2,1)} %param.11) | copy-start | bytes 3145732
  6.5 132.2 %all-gather.2.cloned.1.call-start = ((), (), s32[]{:S(2)}) async-start(), calls=%async_computation | async-start | bytes 17039360 | tf_op jit(solution)/shard_map/all_gather | solution.py:154
  6.5 1.7 %collective-permute-start.12 = (bf16[1024,128]{1,0:T(8,128)(2,1)}, bf16[1024,128]{1,0:T(8,128)(2,1)S(1)}, u32[]{:S(2)}, u32[]{:S(2)}) collective-permute-start(bf16[1024,128]{1,0:T(8,128)(2,1)} %param.19), channel_id=1, source_target_pairs={{0,0},{64,65},{128,130},{192,195},{1,192},{65,1},{129,66},{193,131... | collective-permute-start | bytes 786440 | tf_op jit(solution)/shard_map/ppermute | solution.py:153
  12.1 12.4 %collective-permute-start.1 = (f32[65,128]{1,0:T(8,128)S(1)}, f32[65,128]{1,0:T(8,128)S(1)}, u32[]{:S(2)}, u32[]{:S(2)}) collective-permute-start(f32[65,128]{1,0:T(8,128)S(1)} %select_maximum_fusion), channel_id=1, source_target_pairs={{0,4},{4,0},{1,5},{5,1},{2,6},{6,2},{3,7},{7,3},{8,12},{12,8},{9,1... | collective-permute-start | bytes 99848 | tf_op jit(solution)/shard_map/ppermute | solution.py:99
  23.9 49.6 %copy-start.10 = (u8[512,64]{0,1:T(8,128)(4,1)}, u8[512,64]{0,1:T(8,128)(4,1)S(1)}, u32[]{:S(2)}) copy-start(u8[512,64]{0,1:T(8,128)(4,1)S(1)} %get-tuple-element.48) | copy-start | bytes 98308
  24.5 10.7 %collective-permute-start.8 = (f32[65,128]{1,0:T(8,128)S(1)}, f32[65,128]{1,0:T(8,128)S(1)}, u32[]{:S(2)}, u32[]{:S(2)}) collective-permute-start(f32[65,128]{1,0:T(8,128)S(1)} %fusion.76), channel_id=1, source_target_pairs={{0,56},{8,0},{16,8},{24,16},{32,24},{40,32},{48,40},{56,48},{1,57}... | collective-permute-start | bytes 99848 | tf_op jit(solution)/shard_map/ppermute | solution.py:99
  28.5 8.9 %collective-permute-start.7 = (f32[65,128]{1,0:T(8,128)S(1)}, f32[65,128]{1,0:T(8,128)S(1)}, u32[]{:S(2)}, u32[]{:S(2)}) collective-permute-start(f32[65,128]{1,0:T(8,128)S(1)} %fusion.76), channel_id=1, source_target_pairs={{0,48},{8,56},{16,0},{24,8},{32,16},{40,24},{48,32},{56,40},{1,49}... | collective-permute-start | bytes 99848 | tf_op jit(solution)/shard_map/ppermute | solution.py:99
  30.3 9.1 %collective-permute-start.6 = (f32[65,128]{1,0:T(8,128)S(1)}, f32[65,128]{1,0:T(8,128)S(1)}, u32[]{:S(2)}, u32[]{:S(2)}) collective-permute-start(f32[65,128]{1,0:T(8,128)S(1)} %fusion.76), channel_id=1, source_target_pairs={{0,40},{8,48},{16,56},{24,0},{32,8},{40,16},{48,24},{56,32},{1,41}... | collective-permute-start | bytes 99848 | tf_op jit(solution)/shard_map/ppermute | solution.py:99
  30.8 13.2 %collective-permute-start.5 = (f32[65,128]{1,0:T(8,128)S(1)}, f32[65,128]{1,0:T(8,128)S(1)}, u32[]{:S(2)}, u32[]{:S(2)}) collective-permute-start(f32[65,128]{1,0:T(8,128)S(1)} %fusion.76), channel_id=1, source_target_pairs={{0,32},{8,40},{16,48},{24,56},{32,0},{40,8},{48,16},{56,24},{1,33}... | collective-permute-start | bytes 99848 | tf_op jit(solution)/shard_map/ppermute | solution.py:99
  35.3 8.7 %collective-permute-start.4 = (f32[65,128]{1,0:T(8,128)S(1)}, f32[65,128]{1,0:T(8,128)S(1)}, u32[]{:S(2)}, u32[]{:S(2)}) collective-permute-start(f32[65,128]{1,0:T(8,128)S(1)} %fusion.76), channel_id=1, source_target_pairs={{0,24},{8,32},{16,40},{24,48},{32,56},{40,0},{48,8},{56,16},{1,25}... | collective-permute-start | bytes 99848 | tf_op jit(solution)/shard_map/ppermute | solution.py:99
  35.3 8.7 %collective-permute-start.3 = (f32[65,128]{1,0:T(8,128)S(1)}, f32[65,128]{1,0:T(8,128)S(1)}, u32[]{:S(2)}, u32[]{:S(2)}) collective-permute-start(f32[65,128]{1,0:T(8,128)S(1)} %fusion.76), channel_id=1, source_target_pairs={{0,16},{8,24},{16,32},{24,40},{32,48},{40,56},{48,0},{56,8},{1,17}... | collective-permute-start | bytes 99848 | tf_op jit(solution)/shard_map/ppermute | solution.py:99
  37.4 6.6 %collective-permute-start.2 = (f32[65,128]{1,0:T(8,128)S(1)}, f32[65,128]{1,0:T(8,128)S(1)}, u32[]{:S(2)}, u32[]{:S(2)}) collective-permute-start(f32[65,128]{1,0:T(8,128)S(1)} %fusion.76), channel_id=1, source_target_pairs={{0,8},{8,16},{16,24},{24,32},{32,40},{40,48},{48,56},{56,0},{1,9},... | collective-permute-start | bytes 99848 | tf_op jit(solution)/shard_map/ppermute | solution.py:99
  39.4 38.5 %collective-permute-start = (bf16[512,256]{1,0:T(8,128)(2,1)}, bf16[512,256]{1,0:T(8,128)(2,1)}, u32[]{:S(2)}, u32[]{:S(2)}) collective-permute-start(bf16[512,256]{1,0:T(8,128)(2,1)} %pad_maximum_fusion.1), channel_id=1, source_target_pairs={{0,4},{4,8},{8,12},{12,16},{16,20},{20,24},{24,28},{28,32},{32,36}... | collective-permute-start | bytes 786440 | tf_op jit(solution)/shard_map/ppermute | solution.py:13
  44.0 24.5 %collective-permute-start.11 = (f32[65,128]{1,0:T(8,128)S(1)}, f32[65,128]{1,0:T(8,128)S(1)}, u32[]{:S(2)}, u32[]{:S(2)}) collective-permute-start(f32[65,128]{1,0:T(8,128)S(1)} %add_add_fusion), channel_id=1, source_target_pairs={{0,192},{64,0},{128,64},{192,128},{1,193},{65,1},{129,65},{193,129... | collective-permute-start | bytes 99848 | tf_op jit(solution)/shard_map/ppermute | solution.py:99
  62.8 5.7 %collective-permute-start.10 = (f32[65,128]{1,0:T(8,128)S(1)}, f32[65,128]{1,0:T(8,128)S(1)}, u32[]{:S(2)}, u32[]{:S(2)}) collective-permute-start(f32[65,128]{1,0:T(8,128)S(1)} %add_add_fusion), channel_id=1, source_target_pairs={{0,128},{64,192},{128,0},{192,64},{1,129},{65,193},{129,1},{193,65... | collective-permute-start | bytes 99848 | tf_op jit(solution)/shard_map/ppermute | solution.py:99
  64.5 4.6 %collective-permute-start.9 = (f32[65,128]{1,0:T(8,128)S(1)}, f32[65,128]{1,0:T(8,128)S(1)}, u32[]{:S(2)}, u32[]{:S(2)}) collective-permute-start(f32[65,128]{1,0:T(8,128)S(1)} %add_add_fusion), channel_id=1, source_target_pairs={{0,64},{64,128},{128,192},{192,0},{1,65},{65,129},{129,193},{193,1... | collective-permute-start | bytes 99848 | tf_op jit(solution)/shard_map/ppermute | solution.py:99
  74.7 4.2 %copy-start.5 = (bf16[512,128]{1,0:T(8,128)(2,1)S(1)}, bf16[512,128]{1,0:T(8,128)(2,1)}, u32[]{:S(2)}) copy-start(bf16[512,128]{1,0:T(8,128)(2,1)} %param.12) | copy-start | bytes 393220
  74.7 7.0 %copy-start.6 = (bf16[512,128]{1,0:T(8,128)(2,1)S(1)}, bf16[512,128]{1,0:T(8,128)(2,1)}, u32[]{:S(2)}) copy-start(bf16[512,128]{1,0:T(8,128)(2,1)} %param.13) | copy-start | bytes 393220
  78.9 9.9 %copy-start.4 = (bf16[128,1024]{0,1:T(8,128)(2,1)S(1)}, bf16[128,1024]{0,1:T(8,128)(2,1)}, u32[]{:S(2)}) copy-start(bf16[128,1024]{0,1:T(8,128)(2,1)} %copy.56) | copy-start | bytes 786436
  88.9 1.6 copy-start.3
  94.9 23.9 %collective-permute-start.13 = (bf16[512,1024]{0,1:T(8,128)(2,1)S(1)}, bf16[512,1024]{0,1:T(8,128)(2,1)}, u32[]{:S(2)}, u32[]{:S(2)}) collective-permute-start(bf16[512,1024]{0,1:T(8,128)(2,1)S(1)} %pad_maximum_fusion), channel_id=1, source_target_pairs={{0,1},{1,2},{2,3},{3,0},{4,5},{5,6},{6,7},{7,4},{8,9},{9,10},{10,1... | collective-permute-start | bytes 3145736 | tf_op jit(solution)/shard_map/ppermute | solution.py:161
  96.1 47.6 %collective-permute-start.14 = (bf16[512,1024]{0,1:T(8,128)(2,1)S(1)}, bf16[512,1024]{0,1:T(8,128)(2,1)}, u32[]{:S(2)}, u32[]{:S(2)}) collective-permute-start(bf16[512,1024]{0,1:T(8,128)(2,1)S(1)} %pad_maximum_fusion), channel_id=1, source_target_pairs={{0,2},{1,3},{2,0},{3,1},{4,6},{5,7},{6,4},{7,5},{8,10},{9,11},{10,... | collective-permute-start | bytes 3145736 | tf_op jit(solution)/shard_map/ppermute | solution.py:161
  98.9 54.3 %collective-permute-start.15 = (bf16[512,1024]{0,1:T(8,128)(2,1)S(1)}, bf16[512,1024]{0,1:T(8,128)(2,1)S(1)}, u32[]{:S(2)}, u32[]{:S(2)}) collective-permute-start(bf16[512,1024]{0,1:T(8,128)(2,1)S(1)} %pad_maximum_fusion), channel_id=1, source_target_pairs={{0,3},{1,0},{2,1},{3,2},{4,7},{5,4},{6,5},{7,6},{8,11},{9,8},{10,9... | collective-permute-start | bytes 3145736 | tf_op jit(solution)/shard_map/ppermute | solution.py:161
  (13 other events, 13.4 us)
Sparse Core Ops, SparseCore 0:
  9.9 128.8 all-gather.1
where the time goes:
time: 167 us; the launch traced here: 166 us
  starting transfers between devices  47.7 us (29%)
  waiting for transfers between devices  40.6 us (24%)
  matrix products  34.3 us (21%)
  local copies, waits for them, and re-layouts  16.7 us (10%)
  between operations  14.6 us (9%)
  other arithmetic  12.4 us (7%)
    ppermute x11, starting transfers between devices, body(): lax.ppermute(running, axis, [(i, (i + shift) % size) for i in range(size)])  37.4 us
    dot_general x4, matrix products, body(): jnp.dot(rows_in, gathered[:, shift * width:(shift + 1) * width], preferre...  20.5 us
    all_gather x1, waiting for transfers between devices, body(): gathered = lax.all_gather(moved, CTX, axis=1, tiled=True)  20 us
    ppermute x3, waiting for transfers between devices, body(): lax.ppermute(group_cols, 'tp', [(i, (i + shift) % n_tp) for i in range(n_...  19.9 us
    gather x4, local copies, waits for them, and re-layouts, body(): key_rows = jnp.take(window_keys, chosen, axis=0).reshape(-1, head_dim)  4.78 us
    unnamed x44, local copies, waits for them, and re-layouts  4.56 us
    ppermute x1, starting transfers between devices, passed_along(): return lax.ppermute(block, axis, route)  4.54 us
    gather x4, local copies, waits for them, and re-layouts, body(): value_rows = jnp.take(window_values, chosen, axis=0).reshape(-1, head_dim)  4.01 us
  transfers between devices with their start and end apart: 17, of which 3 were waited for; matrix products, arithmetic and copies ran while one was open for 33% of the time, Pallas kernels for 0%

commit v1 on v0

--- a/solution.py
+++ b/solution.py
@@ -151,7 +151,9 @@
         for rows in range(n_tp)
     ]
     moved = lax.ppermute(out_weight, ("ctx_0", "tp"), swap)
-    gathered = lax.all_gather(moved, CTX, axis=1, tiled=True)
+    gathered = jnp.concatenate(
+        lax.all_to_all(jnp.stack([moved] * lax.axis_size(CTX)), CTX, 0, 0), axis=1
+    )
     width = gathered.shape[1] // n_tp
     summed = None
     for shift in range(n_tp):

time: 167 us -> 504 us (3.02)
  waiting for transfers between devices: 40.6 us -> 377 us
  between operations: 14.6 us -> 1.21 us
  starting transfers between devices: 47.7 us -> 60 us
    ppermute x11, waiting for transfers between devices: 0.67 us -> 343 us  [body(): lax.ppermute(running, axis, [(i, (i + shift) % size) for i in range(size)])]
    all_to_all x0 -> x1, starting transfers between devices: none -> 28.1 us  [body(): lax.all_to_all(jnp.stack([moved] * lax.axis_size(CTX)), CTX, 0, 0)]
    all_gather x1 -> x0, waiting for transfers between devices: 20 us -> none  [body(): gathered = lax.all_gather(moved, CTX, axis=1, tiled=True)]
    ppermute x11, starting transfers between devices: 37.4 us -> 19.9 us  [body(): lax.ppermute(running, axis, [(i, (i + shift) % size) for i in range(size)])]
    ppermute x3, waiting for transfers between devices: 19.9 us -> 34.3 us  [body(): lax.ppermute(group_cols, 'tp', [(i, (i + shift) % n_tp) for i in range(n_...]
    another operation x0 -> x1, local copies, waits for them, and re-layouts: none -> 6.09 us  [body(): jnp.stack([moved] * lax.axis_size(CTX))]
  transfers between devices with their start and end apart: 17 -> 17, of which waited for: 3 -> 5; matrix products, arithmetic and copies ran while one was open for 33% -> 10% of each run, Pallas kernels for 0% -> 0%
where the time goes in v1:
time: 504 us; the launch traced here: 503 us
  waiting for transfers between devices  377 us (75%)
  starting transfers between devices  60 us (12%)
  matrix products  32.9 us (7%)
  local copies, waits for them, and re-layouts  20.5 us (4%)
  other arithmetic  11.3 us (2%)
    ppermute x11, waiting for transfers between devices, body(): lax.ppermute(running, axis, [(i, (i + shift) % size) for i in range(size)])  343 us
    ppermute x3, waiting for transfers between devices, body(): lax.ppermute(group_cols, 'tp', [(i, (i + shift) % n_tp) for i in range(n_...  34.3 us
    all_to_all x1, starting transfers between devices, body(): lax.all_to_all(jnp.stack([moved] * lax.axis_size(CTX)), CTX, 0, 0)  28.1 us
    dot_general x4, matrix products, body(): jnp.dot(rows_in, gathered[:, shift * width:(shift + 1) * width], preferre...  20.5 us
    ppermute x11, starting transfers between devices, body(): lax.ppermute(running, axis, [(i, (i + shift) % size) for i in range(size)])  19.9 us
  transfers between devices with their start and end apart: 17, of which 5 were waited for; matrix products, arithmetic and copies ran while one was open for 10% of the time, Pallas kernels for 0%

profile of v1, /device:TPU:1, one launch (start us, length us, event | category | flops | bytes accessed | tf_op | source)
XLA Modules:
  0.0 503.1 jit_solution(16749012649177767324)
XLA Ops:
  0.0 1.7 collective-permute-start.12
  1.9 6.1 %stack.5 = bf16[64,1024,128]{1,2,0:T(8,128)(2,1)} broadcast(bf16[1024,128]{0,1:T(8,128)(2,1)S(1)} %copy.36), dimensions={1,2} | broadcast | bytes 17039360 | tf_op jit(solution)/shard_map/stack | solution.py:155
  8.0 28.1 %all-to-all-start = ((bf16[64,1024,128]{1,2,0:T(8,128)(2,1)}), bf16[64,1024,128]{1,2,0:T(8,128)(2,1)}, u32[]{:S(2)}, u32[]{:S(2)}) async-start(bf16[64,1024,128]{1,2,0:T(8,128)(2,1)} %stack.5), calls=%async_computation | async-start | bytes 33554432 | tf_op jit(solution)/shard_map/all_to_all | solution.py:155
  46.7 2.1 collective-permute-start.3
  48.8 2.4 collective-permute-start.4
  51.2 2.1 collective-permute-start.5
  53.3 2.4 collective-permute-start.6
  55.7 340.1 %collective-permute-done.2 = f32[65,128]{1,0:T(8,128)S(1)} collective-permute-done((f32[65,128]{1,0:T(8,128)S(1)}, f32[65,128]{1,0:T(8,128)S(1)}, u32[]{:S(2)}, u32[]{:S(2)}) %collective-permute-start.2) | collective-permute-done | bytes 33312 | tf_op jit(solution)/shard_map/ppermute | solution.py:99
  395.8 2.7 collective-permute-start.7
  398.5 2.3 collective-permute-done.3
  400.8 1.9 collective-permute-start.8
  403.0 4.8 collective-permute-start
  407.9 3.1 collective-permute-start.10
  417.8 4.5 fusion.39
  423.5 3.1 fusion.41
  442.7 1.6 collective-permute-start.14
  444.4 2.1 collective-permute-start.13
  446.4 1.7 collective-permute-start.15
  448.2 18.1 %collective-permute-done.14 = bf16[512,1024]{0,1:T(8,128)(2,1)} collective-permute-done((bf16[512,1024]{0,1:T(8,128)(2,1)S(1)}, bf16[512,1024]{0,1:T(8,128)(2,1)}, u32[]{:S(2)}, u32[]{:S(2)}) %collective-permute-start.14) | collective-permute-done | bytes 1048608 | tf_op jit(solution)/shard_map/ppermute | solution.py:163
  466.2 4.9 fusion.2
  471.1 4.6 fusion.6
  475.7 16.3 %collective-permute-done.13 = bf16[512,1024]{0,1:T(8,128)(2,1)} collective-permute-done((bf16[512,1024]{0,1:T(8,128)(2,1)S(1)}, bf16[512,1024]{0,1:T(8,128)(2,1)}, u32[]{:S(2)}, u32[]{:S(2)}) %collective-permute-start.13) | collective-permute-done | bytes 1048608 | tf_op jit(solution)/shard_map/ppermute | solution.py:163
  492.0 4.9 fusion.4
  496.9 6.2 %add_convert_fusion = bf16[512,2048]{1,0:T(8,128)(2,1)} fusion(f32[512,2048]{1,0:T(8,128)S(1)} %fusion.2, f32[512,2048]{1,0:T(8,128)S(1)} %fusion.6, f32[512,2048]{1,0:T(8,128)S(1)} %fusion.4, bf16[512,1024]{0,1:T(8,128)(2,1)S(1)} %collective-permute-done.15, bf16[1024,8192]{0,1:T(8,128)(2,1)} %bitcast.45), kind=kOutput, calls=%fused_computation.16 | convolution fusion | flops 2151677952 | bytes 19922944 | tf_op jit(solution)/shard_map/dot_general | solution.py:164
  (135 shorter events, 34.2 us)
Async XLA Ops:
  0.0 43.6 %copy-start = (bf16[1,128,64]{1,2,0:T(8,128)(2,1)S(1)}, bf16[1,128,64]{1,2,0:T(8,128)(2,1)}, u32[]{:S(2)}) copy-start(bf16[1,128,64]{1,2,0:T(8,128)(2,1)} %param.16) | copy-start | bytes 49156
  0.0 1.7 collective-permute-start.12
  8.0 28.2 %copy-start.22 = (s32[512,1]{0,1:T(1,128)S(1)}, s32[512,1]{0,1:T(1,128)}, u32[]{:S(2)}) copy-start(s32[512,1]{0,1:T(1,128)} %param.14) | copy-start | bytes 6148
  8.0 28.2 %copy-start.6 = (bf16[512,128]{1,0:T(8,128)(2,1)S(1)}, bf16[512,128]{1,0:T(8,128)(2,1)}, u32[]{:S(2)}) copy-start(bf16[512,128]{1,0:T(8,128)(2,1)} %param.12) | copy-start | bytes 393220
  8.0 28.2 %copy-start.23 = (bf16[1,128,64]{1,2,0:T(8,128)(2,1)S(1)}, bf16[1,128,64]{1,2,0:T(8,128)(2,1)}, u32[]{:S(2)}) copy-start(bf16[1,128,64]{1,2,0:T(8,128)(2,1)} %param.17) | copy-start | bytes 49156
  8.0 28.5 %copy-start.7 = (bf16[512,128]{1,0:T(8,128)(2,1)S(1)}, bf16[512,128]{1,0:T(8,128)(2,1)}, u32[]{:S(2)}) copy-start(bf16[512,128]{1,0:T(8,128)(2,1)} %param.13) | copy-start | bytes 393220
  8.0 29.4 %copy-start.17 = (s32[4,2]{0,1:T(2,128)S(1)}, s32[4,2]{0,1:T(2,128)}, u32[]{:S(2)}) copy-start(s32[4,2]{0,1:T(2,128)} %param.15) | copy-start | bytes 100
  8.0 458.2 %all-to-all-start = ((bf16[64,1024,128]{1,2,0:T(8,128)(2,1)}), bf16[64,1024,128]{1,2,0:T(8,128)(2,1)}, u32[]{:S(2)}, u32[]{:S(2)}) async-start(bf16[64,1024,128]{1,2,0:T(8,128)(2,1)} %stack.5), calls=%async_computation | async-start | bytes 33554432 | tf_op jit(solution)/shard_map/all_to_all | solution.py:155
  36.8 8.6 %collective-permute-start.1 = (f32[65,128]{1,0:T(8,128)S(1)}, f32[65,128]{1,0:T(8,128)S(1)}, u32[]{:S(2)}, u32[]{:S(2)}) collective-permute-start(f32[65,128]{1,0:T(8,128)S(1)} %select_maximum_fusion), channel_id=1, source_target_pairs={{0,4},{4,0},{1,5},{5,1},{2,6},{6,2},{3,7},{7,3},{8,12},{12,8},{9,1... | collective-permute-start | bytes 99848 | tf_op jit(solution)/shard_map/ppermute | solution.py:99
  45.4 370.1 %copy-start.15 = (f32[65,128]{1,0:T(8,128)}, f32[65,128]{1,0:T(8,128)S(1)}, u32[]{:S(2)}) copy-start(f32[65,128]{1,0:T(8,128)S(1)} %collective-permute-done.1) | copy-start | bytes 99844
  45.4 350.4 %collective-permute-start.2 = (f32[65,128]{1,0:T(8,128)S(1)}, f32[65,128]{1,0:T(8,128)S(1)}, u32[]{:S(2)}, u32[]{:S(2)}) collective-permute-start(f32[65,128]{1,0:T(8,128)S(1)} %fusion.76), channel_id=1, source_target_pairs={{0,8},{8,16},{16,24},{24,32},{32,40},{40,48},{48,56},{56,0},{1,9},... | collective-permute-start | bytes 99848 | tf_op jit(solution)/shard_map/ppermute | solution.py:99
  46.7 354.1 %collective-permute-start.3 = (f32[65,128]{1,0:T(8,128)S(1)}, f32[65,128]{1,0:T(8,128)S(1)}, u32[]{:S(2)}, u32[]{:S(2)}) collective-permute-start(f32[65,128]{1,0:T(8,128)S(1)} %fusion.76), channel_id=1, source_target_pairs={{0,16},{8,24},{16,32},{24,40},{32,48},{40,56},{48,0},{56,8},{1,17}... | collective-permute-start | bytes 99848 | tf_op jit(solution)/shard_map/ppermute | solution.py:99
  48.8 354.2 %collective-permute-start.4 = (f32[65,128]{1,0:T(8,128)S(1)}, f32[65,128]{1,0:T(8,128)S(1)}, u32[]{:S(2)}, u32[]{:S(2)}) collective-permute-start(f32[65,128]{1,0:T(8,128)S(1)} %fusion.76), channel_id=1, source_target_pairs={{0,24},{8,32},{16,40},{24,48},{32,56},{40,0},{48,8},{56,16},{1,25}... | collective-permute-start | bytes 99848 | tf_op jit(solution)/shard_map/ppermute | solution.py:99
  51.2 356.6 %collective-permute-start.5 = (f32[65,128]{1,0:T(8,128)S(1)}, f32[65,128]{1,0:T(8,128)S(1)}, u32[]{:S(2)}, u32[]{:S(2)}) collective-permute-start(f32[65,128]{1,0:T(8,128)S(1)} %fusion.76), channel_id=1, source_target_pairs={{0,32},{8,40},{16,48},{24,56},{32,0},{40,8},{48,16},{56,24},{1,33}... | collective-permute-start | bytes 99848 | tf_op jit(solution)/shard_map/ppermute | solution.py:99
  53.3 354.5 %collective-permute-start.6 = (f32[65,128]{1,0:T(8,128)S(1)}, f32[65,128]{1,0:T(8,128)S(1)}, u32[]{:S(2)}, u32[]{:S(2)}) collective-permute-start(f32[65,128]{1,0:T(8,128)S(1)} %fusion.76), channel_id=1, source_target_pairs={{0,40},{8,48},{16,56},{24,0},{32,8},{40,16},{48,24},{56,32},{1,41}... | collective-permute-start | bytes 99848 | tf_op jit(solution)/shard_map/ppermute | solution.py:99
  395.8 12.0 %collective-permute-start.7 = (f32[65,128]{1,0:T(8,128)S(1)}, f32[65,128]{1,0:T(8,128)S(1)}, u32[]{:S(2)}, u32[]{:S(2)}) collective-permute-start(f32[65,128]{1,0:T(8,128)S(1)} %fusion.76), channel_id=1, source_target_pairs={{0,48},{8,56},{16,0},{24,8},{32,16},{40,24},{48,32},{56,40},{1,49}... | collective-permute-start | bytes 99848 | tf_op jit(solution)/shard_map/ppermute | solution.py:99
  400.8 7.0 %collective-permute-start.8 = (f32[65,128]{1,0:T(8,128)S(1)}, f32[65,128]{1,0:T(8,128)S(1)}, u32[]{:S(2)}, u32[]{:S(2)}) collective-permute-start(f32[65,128]{1,0:T(8,128)S(1)} %fusion.76), channel_id=1, source_target_pairs={{0,56},{8,0},{16,8},{24,16},{32,24},{40,32},{48,40},{56,48},{1,57}... | collective-permute-start | bytes 99848 | tf_op jit(solution)/shard_map/ppermute | solution.py:99
  403.0 23.7 %collective-permute-start = (bf16[512,256]{1,0:T(8,128)(2,1)}, bf16[512,256]{1,0:T(8,128)(2,1)}, u32[]{:S(2)}, u32[]{:S(2)}) collective-permute-start(bf16[512,256]{1,0:T(8,128)(2,1)} %pad_maximum_fusion.1), channel_id=1, source_target_pairs={{0,4},{4,8},{8,12},{12,16},{16,20},{20,24},{24,28},{28,32},{32,36}... | collective-permute-start | bytes 786440 | tf_op jit(solution)/shard_map/ppermute | solution.py:13
  407.9 8.5 %collective-permute-start.10 = (f32[65,128]{1,0:T(8,128)S(1)}, f32[65,128]{1,0:T(8,128)S(1)}, u32[]{:S(2)}, u32[]{:S(2)}) collective-permute-start(f32[65,128]{1,0:T(8,128)S(1)} %add_add_fusion), channel_id=1, source_target_pairs={{0,128},{64,192},{128,0},{192,64},{1,129},{65,193},{129,1},{193,65... | collective-permute-start | bytes 99848 | tf_op jit(solution)/shard_map/ppermute | solution.py:99
  410.9 5.4 %collective-permute-start.11 = (f32[65,128]{1,0:T(8,128)S(1)}, f32[65,128]{1,0:T(8,128)S(1)}, u32[]{:S(2)}, u32[]{:S(2)}) collective-permute-start(f32[65,128]{1,0:T(8,128)S(1)} %add_add_fusion), channel_id=1, source_target_pairs={{0,192},{64,0},{128,64},{192,128},{1,193},{65,1},{129,65},{193,129... | collective-permute-start | bytes 99848 | tf_op jit(solution)/shard_map/ppermute | solution.py:99
  412.4 4.0 collective-permute-start.9
  442.7 23.5 %collective-permute-start.14 = (bf16[512,1024]{0,1:T(8,128)(2,1)S(1)}, bf16[512,1024]{0,1:T(8,128)(2,1)}, u32[]{:S(2)}, u32[]{:S(2)}) collective-permute-start(bf16[512,1024]{0,1:T(8,128)(2,1)S(1)} %pad_maximum_fusion), channel_id=1, source_target_pairs={{0,2},{1,3},{2,0},{3,1},{4,6},{5,7},{6,4},{7,5},{8,10},{9,11},{10,... | collective-permute-start | bytes 3145736 | tf_op jit(solution)/shard_map/ppermute | solution.py:163
  444.4 47.6 %collective-permute-start.13 = (bf16[512,1024]{0,1:T(8,128)(2,1)S(1)}, bf16[512,1024]{0,1:T(8,128)(2,1)}, u32[]{:S(2)}, u32[]{:S(2)}) collective-permute-start(bf16[512,1024]{0,1:T(8,128)(2,1)S(1)} %pad_maximum_fusion), channel_id=1, source_target_pairs={{0,1},{1,2},{2,3},{3,0},{4,5},{5,6},{6,7},{7,4},{8,9},{9,10},{10,1... | collective-permute-start | bytes 3145736 | tf_op jit(solution)/shard_map/ppermute | solution.py:163
  446.4 50.5 %collective-permute-start.15 = (bf16[512,1024]{0,1:T(8,128)(2,1)S(1)}, bf16[512,1024]{0,1:T(8,128)(2,1)S(1)}, u32[]{:S(2)}, u32[]{:S(2)}) collective-permute-start(bf16[512,1024]{0,1:T(8,128)(2,1)S(1)} %pad_maximum_fusion), channel_id=1, source_target_pairs={{0,3},{1,0},{2,1},{3,2},{4,7},{5,4},{6,5},{7,6},{8,11},{9,8},{10,9... | collective-permute-start | bytes 3145736 | tf_op jit(solution)/shard_map/ppermute | solution.py:163
  (17 other events, 52.8 us)
